TPU v7x, 32 devices: a whole 2x2x4 slice. The times are simulated.
32 devices in a mesh: row: 4 (over y, core), col: 8 (over z, x).
Axes of the slice: x: 2, y: 2, z: 4, core: 2. Of those that a mesh axis runs over, the one named last changes fastest.
Arguments:
- hess: bfloat16 [10, 4, 256, 5, 8, 256], P(None, 'row', None, None, 'col'), may hold values from -6 to 6
- coupling: float32 [32, 256, 2, 256], P(('row', 'col')), may hold values from -6 to 6
- dest_row: int32 [32, 256, 1], P(('row', 'col')), may hold values from 0 to 3, as said below
- local_row: int32 [32, 256], P(('row', 'col')), may hold values from 256 to 2559
- live: int32 [32], P(('row', 'col')), may hold values from 1 to 256, 6144 in all
- pattern: int32 [40, 40], replicated, may hold values 0 or 1
Outputs:
- factor: float32 [10, 4, 256, 5, 8, 256], P(None, 'row', None, None, 'col')
Inputs may be any that keep to these rules, and one draw needn't show every extreme that they name: `dest_row`: among one owner's 256 slots, used or not, one grid row is named exactly 64 times and no grid row more than 64 times. The first live[d] slots of owner d are used; the counts sum to 6144 and one owner uses all 256.
All inputs are finite; a program needn't handle non-finite values. No bound on the sum of `live` on one device may be relied on, other than what follows from the above.
Results may differ from a plain program's by a relative error of at most 0.0003.
Values sent between devices are 32-bit elements; how exact they have to be, the bound alone decides.
No kernel may reach another device: no remote copies, remote signals or barrier semaphores. Data moves between devices by JAX's collectives and lax.ppermute only.
A program may use at most 192 MiB of HBM per device.

v0:
```python
import jax
import jax.numpy as jnp
from jax import lax
from jax.sharding import PartitionSpec as P


def broadcast(value, axis, source):
    kept = jnp.where(lax.axis_index(axis) == source, value, 0).astype(value.dtype)
    return lax.psum(kept, axis)


def symmetric(block):
    return jnp.tril(block) + jnp.swapaxes(jnp.tril(block, -1), -1, -2)


def right_solve(rows, lower_factor):
    return jax.scipy.linalg.solve_triangular(lower_factor, rows.T, lower=True).T


def leading(block00, block10, block11, link):
    size = block00.shape[0]
    first = symmetric(block00)
    second = symmetric(block11)
    coupled = link * block10
    whole = jnp.concatenate(
        [jnp.concatenate([first, coupled.T], 1), jnp.concatenate([coupled, second], 1)], 0
    )
    ident = jnp.eye(2 * size, dtype=whole.dtype)
    spread = jnp.sum(jnp.abs(whole), axis=1) - jnp.abs(jnp.diagonal(whole))
    whole = whole * (1.0 - ident) + ident * (1.0 + spread)[:, None]
    factor00 = jnp.linalg.cholesky(whole[:size, :size])
    factor10 = right_solve(whole[size:, :size], factor00)
    reduced = whole[size:, size:] - jnp.dot(factor10, factor10.T, precision=lax.Precision.HIGHEST)
    factor11 = jnp.linalg.cholesky(reduced)
    return (factor00, factor10, factor11)


def solve_rows(rows, lower_factor):
    result = right_solve(rows, lower_factor)
    return result


def panel_solve(block_rows, f00, f10, f11):
    first = solve_rows(block_rows[:, 0], f00)
    second = solve_rows(
        block_rows[:, 1] - jnp.dot(first, f10.T, precision=lax.Precision.HIGHEST), f11
    )
    return jnp.stack([first, second], 1)


def shards(hess, coupling, dest_row, local_row, live, pattern):
    grid_rows = lax.axis_size("row")
    grid_cols = lax.axis_size("col")
    here_row = lax.axis_index("row")
    here_col = lax.axis_index("col")
    row_blocks = hess.shape[0]
    col_blocks = hess.shape[3]
    block = hess.shape[2]
    slot_count = coupling.shape[1]
    bucket = slot_count // 4
    height = row_blocks * block
    mask = pattern.astype(jnp.float32)
    grid_ids = jnp.arange(grid_rows, dtype=jnp.int32)
    dest = dest_row[0, :, 0]
    active = jnp.arange(slot_count, dtype=jnp.int32) < live[0]
    hits = (dest[:, None] == grid_ids[None, :]) & active[:, None]
    ranks = jnp.cumsum(hits.astype(jnp.int32), axis=0) - 1
    place = jnp.sum(jnp.where(hits, ranks + grid_ids[None, :] * bucket, 0), axis=1)
    place = jnp.where(active, place, grid_rows * bucket)
    outgoing = (
        jnp.zeros((grid_rows * bucket, 2, block), jnp.float32)
        .at[place]
        .set(coupling[0], mode="drop")
    )
    labels = (
        jnp.zeros((grid_rows * bucket,), jnp.float32)
        .at[place]
        .set(local_row[0].astype(jnp.float32), mode="drop")
    )
    arrived, arrived_rows = (
        lax.all_to_all(
            outgoing.reshape(grid_rows, bucket, 2, block),
            "row",
            split_axis=0,
            concat_axis=0,
            tiled=True,
        ),
        lax.all_to_all(
            labels.reshape(grid_rows, bucket), "row", split_axis=0, concat_axis=0, tiled=True
        ),
    )
    partial_value = (
        jnp.zeros((height, 2, block), jnp.float32)
        .at[arrived_rows.astype(jnp.int32).reshape(-1)]
        .add(arrived.reshape(-1, 2, block))
    )
    own = hess[:, 0, :, 0, 0, :].astype(jnp.float32).reshape(height, block)
    which = (jnp.arange(2, dtype=jnp.int32) == here_col).astype(jnp.float32)
    partial_value = partial_value + own[:, None, :] * which[None, :, None]
    corner = hess[0, 0, :, 0, 0, :].astype(jnp.float32)
    at_first = ((here_row == 0) & (here_col == 0)).astype(jnp.float32)
    at_below = ((here_row == 1) & (here_col == 0)).astype(jnp.float32)
    at_second = ((here_row == 1) & (here_col == 1)).astype(jnp.float32)
    pivots = lax.psum(
        jnp.stack([at_first * corner, at_below * corner, at_second * corner]), ("row", "col")
    )
    f00, f10, f11 = leading(pivots[0], pivots[1], pivots[2], mask[1, 0])
    mine = lax.dynamic_index_in_dim(
        mask.reshape(row_blocks, grid_rows, -1), here_row, 1, keepdims=False
    )
    rowmask = jnp.repeat(mine[:, :2], block, axis=0)
    summed = lax.psum(partial_value, "col")
    panel = panel_solve(summed * rowmask[:, :, None], f00, f10, f11)
    head_first = jnp.where(here_row == 0, f00, f10)
    head_second = jnp.where(here_row == 0, jnp.zeros_like(f11), f11)
    head = jnp.stack([head_first, head_second], 1)
    panel = panel.at[:block].set(jnp.where(here_row < 2, head, panel[:block]))
    ratio = grid_cols // grid_rows
    picked = lax.dynamic_index_in_dim(
        panel.reshape(col_blocks, ratio, block, 2, block), here_col // grid_rows, 1, keepdims=False
    )
    across = broadcast(picked, "row", here_col % grid_rows)
    left = panel.reshape(height, 2 * block)
    right = across.reshape(col_blocks * block, 2 * block)
    update = jnp.dot(left, right.T, precision=lax.Precision.HIGHEST).reshape(
        row_blocks, block, col_blocks, block
    )
    tiles = jnp.transpose(hess[:, 0, :, :, 0, :].astype(jnp.float32), (0, 2, 1, 3))
    sym = symmetric(tiles)
    block_i = jnp.arange(row_blocks, dtype=jnp.int32) * grid_rows + here_row
    block_j = jnp.arange(col_blocks, dtype=jnp.int32) * grid_cols + here_col
    links = lax.dynamic_index_in_dim(
        lax.dynamic_index_in_dim(
            mask.reshape(row_blocks, grid_rows, col_blocks, grid_cols), here_row, 1, keepdims=False
        ),
        here_col,
        2,
        keepdims=False,
    )
    same = (block_i[:, None] == block_j[None, :])[:, :, None, None]
    below = (block_i[:, None] > block_j[None, :])[:, :, None, None]
    base = jnp.where(same, sym, jnp.where(below, links[:, :, None, None] * tiles, 0.0))
    trail = base - jnp.transpose(update, (0, 2, 1, 3))
    lower_panel = jnp.transpose(panel.reshape(row_blocks, block, 2, block), (0, 2, 1, 3))
    panel_tile = lax.dynamic_index_in_dim(lower_panel, jnp.minimum(here_col, 1), 1, keepdims=False)
    in_panel = (block_j < 2)[None, :, None, None]
    kept = (block_i[:, None] >= block_j[None, :])[:, :, None, None]
    result = jnp.where(in_panel, panel_tile[:, None], jnp.where(kept, trail, 0.0))
    return jnp.transpose(result, (0, 2, 1, 3)).reshape(row_blocks, 1, block, col_blocks, 1, block)


def solution(mesh):
    return jax.shard_map(
        shards,
        mesh=mesh,
        in_specs=(
            P(None, "row", None, None, "col", None),
            P(("row", "col"), None, None, None),
            P(("row", "col"), None, None),
            P(("row", "col"), None),
            P(("row", "col")),
            P(),
        ),
        out_specs=P(None, "row", None, None, "col", None),
        check_vma=False,
    )
```

profile of v0, /device:TPU:0, one launch (start us, length us, event | category | flops | bytes accessed | tf_op | source)
XLA Modules:
  0.0 492.9 jit_solution(16189000699029080055)
XLA Ops:
  19.1 9.4 %copy.100 = bf16[10,1,256,5,1,256]{2,5,3,0,4,1:T(8,128)(2,1)} copy(bf16[10,1,256,5,1,256]{5,2,4,3,1,0:T(8,128)(2,1)} %param.11) | data formatting | bytes 13107200 | tf_op args[0]
  39.7 24.2 %scatter_fusion = f32[256,2,256]{2,1,0:T(2,128)} fusion(f32[256,2,256]{2,1,0:T(2,128)} %broadcast_in_dim.117, s32[256]{0:T(256)S(1)} %bitcast.222, f32[256,2,256]{2,1,0:T(2,128)S(1)} %bitcast.212), kind=kCustom, calls=%fused_computation.2 | custom fusion | bytes 1573888 | tf_op jit(solution)/shard_map/scatter | solution.py:73
  67.5 8.7 %all-to-all-done.1 = f32[4,64,2,256]{3,2,1,0:T(2,128)S(1)} async-done(((f32[4,64,2,256]{3,2,1,0:T(2,128)}), f32[4,64,2,256]{3,2,1,0:T(2,128)S(1)}, u32[]{:S(2)}, u32[]{:S(2)}) %all-to-all-start.1) | async-done | bytes 524320 | tf_op jit(solution)/shard_map/all_to_all | solution.py:81
  76.2 30.9 %scatter_fusion.1 = f32[2560,2,256]{2,1,0:T(2,128)} fusion(f32[2560,2,256]{2,1,0:T(2,128)} %broadcast_multiply_fusion.1, s32[256]{0:T(256)S(1)} %bitcast.223, f32[256,2,256]{2,1,0:T(2,128)S(1)} %bitcast.211), kind=kCustom, calls=%fused_computation.3 | custom fusion | flops 131072 | bytes 1573888 | tf_op jit(solution)/shard_map/scatter-add | solution.py:95
  107.1 8.8 %copy.88 = f32[2560,2,256]{0,2,1:T(8,128)} copy(f32[2560,2,256]{2,1,0:T(2,128)} %scatter_fusion.1) | data formatting | bytes 10485760 | tf_op jit(solution)/shard_map/scatter-add | solution.py:95
  116.1 39.1 %all-reduce.5.cloned.1.call-done = f32[3,256,256]{2,1,0:T(8,128)} async-done(((f32[3,256,256]{2,1,0:T(8,128)}), f32[3,256,256]{2,1,0:T(8,128)}) %all-reduce.5.cloned.1.call-update) | async-done | bytes 786448 | tf_op jit(solution)/shard_map/psum | solution.py:104
  158.8 4.5 gather_fusion
  163.8 11.7 %cholesky.130 = f32[128,128]{1,0:T(8,128)S(1)} custom-call(f32[128,128]{1,0:T(8,128)S(1)} %cholesky.194), custom_call_target="Cholesky" | custom-call | tf_op jit(solution)/shard_map/jit(cholesky)/cholesky | solution.py:31
  175.5 9.8 %custom-call.20 = f32[1,128,128]{1,2,0:T(8,128)S(1)} custom-call(f32[1,128,128]{2,1,0:T(8,128)S(1)} %get-tuple-element.87), custom_call_target="InvertDiagBlocksLowerTriangular" | custom-call | tf_op jit(solution)/shard_map/jit(cholesky)/cholesky | solution.py:31
  185.8 11.7 %cholesky.147 = f32[128,128]{1,0:T(8,128)S(1)} custom-call(f32[128,128]{1,0:T(8,128)S(1)} %convolution_subtract_fusion.6), custom_call_target="Cholesky" | custom-call | tf_op jit(solution)/shard_map/jit(cholesky)/cholesky | solution.py:31
  203.4 20.1 %custom-call.21 = f32[2,128,128]{1,2,0:T(8,128)S(1)} custom-call(f32[2,128,128]{2,1,0:T(8,128)S(1)} %get-tuple-element.41), custom_call_target="InvertDiagBlocksLowerTriangular" | custom-call | tf_op jit(solution)/shard_map/jit(_solve_triangular)/triangular_solve | solution.py:17
  225.2 11.7 %cholesky.164 = f32[128,128]{1,0:T(8,128)S(1)} custom-call(f32[128,128]{1,0:T(8,128)S(1)} %cholesky.197), custom_call_target="Cholesky" | custom-call | tf_op jit(solution)/shard_map/jit(cholesky)/cholesky | solution.py:34
  237.0 9.8 %custom-call.22 = f32[1,128,128]{1,2,0:T(8,128)S(1)} custom-call(f32[1,128,128]{2,1,0:T(8,128)S(1)} %get-tuple-element.83), custom_call_target="InvertDiagBlocksLowerTriangular" | custom-call | tf_op jit(solution)/shard_map/jit(cholesky)/cholesky | solution.py:34
  247.3 11.7 %cholesky.181 = f32[128,128]{1,0:T(8,128)S(1)} custom-call(f32[128,128]{1,0:T(8,128)S(1)} %convolution_subtract_fusion.5), custom_call_target="Cholesky" | custom-call | tf_op jit(solution)/shard_map/jit(cholesky)/cholesky | solution.py:34
  266.1 20.5 %custom-call.23 = f32[2,128,128]{1,2,0:T(8,128)} custom-call(f32[2,128,128]{2,1,0:T(8,128)S(1)} %get-tuple-element.42), custom_call_target="InvertDiagBlocksLowerTriangular" | custom-call | tf_op jit(solution)/shard_map/jit(_solve_triangular)/triangular_solve | solution.py:17
  287.3 54.9 %all-reduce.7.cloned.1.call-done = f32[2560,2,256]{0,2,1:T(8,128)} async-done(((f32[2560,2,256]{0,2,1:T(8,128)}), f32[2560,2,256]{0,2,1:T(8,128)}) %all-reduce.7.cloned.1.call-update) | async-done | bytes 5242896 | tf_op jit(solution)/shard_map/psum | solution.py:112
  355.1 4.4 fusion.8
  380.6 11.4 %convert_multiply_fusion = (f32[10,256,5,256]{1,3,2,0:T(8,128)}, f32[10,256,5,256]{1,3,2,0:T(8,128)}) fusion(bf16[10,1,256,5,1,256]{2,5,3,0,4,1:T(8,128)(2,1)} %copy.100, f32[10,5]{1,0:T(8,128)S(1)} %bitcast.215, pred[256,256]{0,1:T(8,128)(4,1)S(1)} %copy-done.9), kind=kLoop, calls=%fused_computation.8 | loop fusion | flops 9830400 | bytes 32833736 | tf_op jit(solution)/shard_map/mul | solution.py:142
  392.0 14.0 %copy.102 = f32[10,256,5,256]{3,1,2,0:T(8,128)} copy(f32[10,256,5,256]{1,3,2,0:T(8,128)} %get-tuple-element.67) | data formatting | bytes 26214400 | tf_op jit(solution)/shard_map/jit(tril)/select_n | solution.py:13
  406.0 14.1 %copy.105 = f32[10,256,5,256]{3,1,2,0:T(8,128)} copy(f32[10,256,5,256]{1,3,2,0:T(8,128)} %get-tuple-element.66) | data formatting | bytes 26214400 | tf_op jit(solution)/shard_map/mul | solution.py:142
  420.3 10.4 %copy.106 = f32[2560,2,256]{2,1,0:T(2,128)} copy(f32[2560,2,256]{2,0,1:T(8,128)} %copy-done) | data formatting | bytes 10485760 | tf_op jit(solution)/shard_map/scatter | solution.py:117
  430.7 8.0 %reshape.409 = f32[10,256,512,1]{2,1,0,3:T(8,128)} reshape(f32[2560,2,256]{2,1,0:T(2,128)} %copy.106) | data formatting | bytes 10485760 | tf_op jit(solution)/shard_map/dot_general | solution.py:125
  440.8 30.4 %fusion.6 = f32[10,1,256,5,1,256]{5,2,3,0,4,1:T(8,128)S(1)} fusion(f32[10,256,5,256]{3,1,2,0:T(8,128)} %copy.102, f32[10,256,5,256]{3,1,2,0:T(8,128)} %copy.105, bf16[10,1,256,5,1,256]{2,5,3,0,4,1:T(8,128)(2,1)} %copy.100, f32[10,256,256]{2,1,0:T(8,128)S(1)} %dynamic-slice_bitcast_fusion, pred[5]{0:T(512)(128)(4,1)S(1)} %broadcast_compare_fusion.3, ...), kind=kOutput, calls=%fused_computation.17 | convolution fusion | flops 20158873600 | bytes 56426652 | tf_op jit(solution)/shard_map/dot_general | solution.py:125
  471.2 15.0 %copy.108 = f32[10,1,256,5,1,256]{5,4,3,2,1,0:T(1,128)} copy(f32[10,1,256,5,1,256]{5,2,3,0,4,1:T(8,128)S(1)} %fusion.6) | data formatting | bytes 26214400 | tf_op jit(solution)/shard_map/reshape | solution.py:149
  (152 shorter events, 88.2 us)
Async XLA Ops:
  13.0 50.9 %all-to-all-start = ((f32[4,1,64]{2,1,0:T(1,128)}), f32[4,1,64]{2,1,0:T(1,128)S(1)}, u32[]{:S(2)}, u32[]{:S(2)}) async-start(f32[4,1,64]{2,1,0:T(1,128)} %all_to_all.9), calls=%async_computation | async-start | bytes 4096 | tf_op jit(solution)/shard_map/all_to_all | solution.py:88
  17.2 138.0 %all-reduce.5.cloned.1.call-start = ((), (), s32[]{:S(2)}) async-start(), calls=%async_computation.2 | async-start | bytes 1572864 | tf_op jit(solution)/shard_map/psum | solution.py:104
  28.6 2.5 copy-start.11
  33.5 6.2 %copy-start.8 = (f32[1,256,2,256]{3,2,1,0:T(2,128)S(1)}, f32[1,256,2,256]{3,2,1,0:T(2,128)}, u32[]{:S(2)}) copy-start(f32[1,256,2,256]{3,2,1,0:T(2,128)} %param.12) | copy-start | bytes 1572868
  63.8 12.3 %all-to-all-start.1 = ((f32[4,64,2,256]{3,2,1,0:T(2,128)}), f32[4,64,2,256]{3,2,1,0:T(2,128)S(1)}, u32[]{:S(2)}, u32[]{:S(2)}) async-start(f32[4,64,2,256]{3,2,1,0:T(2,128)} %bitcast.26), calls=%async_computation.1 | async-start | bytes 1048576 | tf_op jit(solution)/shard_map/all_to_all | solution.py:81
  67.4 274.8 %all-reduce.7.cloned.1.call-start = ((), (), s32[]{:S(2)}) async-start(), calls=%async_computation.3 | async-start | bytes 10485760 | tf_op jit(solution)/shard_map/psum | solution.py:112
  115.9 324.9 %all-reduce.9.cloned.1.call-start = ((), (), s32[]{:S(2)}) async-start(), calls=%async_computation.4 | async-start | bytes 5242880 | tf_op jit(solution)/shard_map/psum | solution.py:9
  155.2 3.2 copy-start.5
  345.2 2.4 copy-start.1
  355.1 4.4 copy-start.10
  360.8 1.1 copy-start.2
  367.0 1.3 copy-start.4
  368.4 2.4 copy-start.3
  371.0 1.0 copy-start.6
  371.0 1.0 copy-start.7
  372.1 2.4 copy-start
  379.7 0.8 copy-start.9
Sparse Core Ops, SparseCore 0:
  23.2 131.9 all-reduce.4
  158.9 183.2 all-reduce.6
  379.9 58.9 all-reduce.8
where the time goes:
time: 500 us; the launch traced here: 493 us
  other arithmetic  172 us (34%)
  local copies, waits for them, and re-layouts  143 us (29%)
  waiting for transfers between devices  103 us (21%)
  matrix products  50.3 us (10%)
  between operations  17 us (3%)
  starting transfers between devices  8.02 us (2%)
    psum x1, waiting for transfers between devices, shards(): summed = lax.psum(partial_value, 'col')  54.9 us
    another operation x5, other arithmetic, right_solve(): return jax.scipy.linalg.solve_triangular(lower_factor, rows.T, lower=True).T  40.6 us
    psum x1, waiting for transfers between devices, shards(): lax.psum(jnp.stack([at_first * corner, at_below * corner, at_second * cor...  39.1 us
    another operation x7, other arithmetic, leading(): factor11 = jnp.linalg.cholesky(reduced)  34.6 us
    another operation x6, other arithmetic, leading(): factor00 = jnp.linalg.cholesky(whole[:size, :size])  33.9 us
    scatter-add x1, other arithmetic, shards(): partial_value = jnp.zeros((height, 2, block), jnp.float32).at[arrived_row...  30.9 us
    dot_general x1, matrix products, shards(): jnp.dot(left, right.T, precision=lax.Precision.HIGHEST)  30.4 us
    scatter x1, local copies, waits for them, and re-layouts, shards(): outgoing = jnp.zeros((grid_rows * bucket, 2, block), jnp.float32).at[plac...  24.2 us
  transfers between devices with their start and end apart: 5, of which 3 were waited for; matrix products, arithmetic and copies ran while one was open for 56% of the time, Pallas kernels for 0%

commit v1 on v0

--- a/solution.py
+++ b/solution.py
@@ -101,9 +101,8 @@
     at_first = ((here_row == 0) & (here_col == 0)).astype(jnp.float32)
     at_below = ((here_row == 1) & (here_col == 0)).astype(jnp.float32)
     at_second = ((here_row == 1) & (here_col == 1)).astype(jnp.float32)
-    pivots = lax.psum(
-        jnp.stack([at_first * corner, at_below * corner, at_second * corner]), ("row", "col")
-    )
+    packet = jnp.stack([at_first * corner, at_below * corner, at_second * corner])
+    pivots = jnp.sum(lax.all_gather(packet, ("row", "col")), axis=0)
     f00, f10, f11 = leading(pivots[0], pivots[1], pivots[2], mask[1, 0])
     mine = lax.dynamic_index_in_dim(
         mask.reshape(row_blocks, grid_rows, -1), here_row, 1, keepdims=False

time: 500 us -> 677 us (1.35)
  waiting for transfers between devices: 103 us -> 263 us
    psum x1, waiting for transfers between devices: 54.9 us -> 258 us  [shards(): summed = lax.psum(partial_value, 'col')]
    psum x1 -> x0, waiting for transfers between devices: 39.1 us -> none  [shards(): lax.psum(jnp.stack([at_first * corner, at_below * corner, at_second * cor...]
    reduce_sum x0 -> x1, other arithmetic: none -> 9.24 us  [shards(): pivots = jnp.sum(lax.all_gather(packet, ('row', 'col')), axis=0)]
    unnamed x28 -> x30, local copies, waits for them, and re-layouts: 17.6 us -> 16.9 us
  transfers between devices with their start and end apart: 5 -> 5, of which waited for: 3 -> 2; matrix products, arithmetic and copies ran while one was open for 56% -> 16% of each run, Pallas kernels for 0% -> 0%
where the time goes in v1:
time: 677 us; the launch traced here: 669 us
  waiting for transfers between devices  263 us (39%)
  other arithmetic  177 us (26%)
  local copies, waits for them, and re-layouts  145 us (21%)
  matrix products  56.9 us (8%)
  between operations  19.1 us (3%)
  starting transfers between devices  7.88 us (1%)
    psum x1, waiting for transfers between devices, shards(): summed = lax.psum(partial_value, 'col')  258 us
    another operation x5, other arithmetic, right_solve(): return jax.scipy.linalg.solve_triangular(lower_factor, rows.T, lower=True).T  40.6 us
    another operation x7, other arithmetic, leading(): factor11 = jnp.linalg.cholesky(reduced)  34.7 us
    another operation x6, other arithmetic, leading(): factor00 = jnp.linalg.cholesky(whole[:size, :size])  34 us
    scatter-add x1, other arithmetic, shards(): partial_value = jnp.zeros((height, 2, block), jnp.float32).at[arrived_row...  30.9 us
    dot_general x1, matrix products, shards(): jnp.dot(left, right.T, precision=lax.Precision.HIGHEST)  30.2 us
    scatter x1, local copies, waits for them, and re-layouts, shards(): outgoing = jnp.zeros((grid_rows * bucket, 2, block), jnp.float32).at[plac...  24.2 us
    another operation x9, matrix products, right_solve(): return jax.scipy.linalg.solve_triangular(lower_factor, rows.T, lower=True).T  17 us
  transfers between devices with their start and end apart: 5, of which 2 were waited for; matrix products, arithmetic and copies ran while one was open for 16% of the time, Pallas kernels for 0%

profile of v1, /device:TPU:0, one launch (start us, length us, event | category | flops | bytes accessed | tf_op | source)
XLA Modules:
  0.0 668.6 jit_solution(15550777185528799908)
XLA Ops:
  20.7 24.2 %scatter_fusion = f32[256,2,256]{2,1,0:T(2,128)} fusion(f32[256,2,256]{2,1,0:T(2,128)} %broadcast_in_dim.117, s32[256]{0:T(256)S(1)} %bitcast.224, f32[256,2,256]{2,1,0:T(2,128)S(1)} %bitcast.214), kind=kCustom, calls=%fused_computation.2 | custom fusion | bytes 1573888 | tf_op jit(solution)/shard_map/scatter | solution.py:73
  52.7 4.5 all-to-all-done.1
  57.2 30.9 %scatter_fusion.1 = f32[2560,2,256]{2,1,0:T(2,128)} fusion(f32[2560,2,256]{2,1,0:T(2,128)} %broadcast_multiply_fusion.1, s32[256]{0:T(256)S(1)} %bitcast.225, f32[256,2,256]{2,1,0:T(2,128)S(1)} %bitcast.213), kind=kCustom, calls=%fused_computation.3 | custom fusion | flops 131072 | bytes 1573888 | tf_op jit(solution)/shard_map/scatter-add | solution.py:95
  88.1 8.8 %copy.88 = f32[2560,2,256]{0,2,1:T(8,128)} copy(f32[2560,2,256]{2,1,0:T(2,128)} %scatter_fusion.1) | data formatting | bytes 10485760 | tf_op jit(solution)/shard_map/scatter-add | solution.py:95
  99.7 9.7 %copy.100 = bf16[10,1,256,5,1,256]{2,5,3,0,4,1:T(8,128)(2,1)} copy(bf16[10,1,256,5,1,256]{5,2,4,3,1,0:T(8,128)(2,1)} %param.11) | data formatting | bytes 13107200 | tf_op args[0]
  110.7 258.1 %all-reduce.4.cloned.1.call-done = f32[2560,2,256]{0,2,1:T(8,128)} async-done(((f32[2560,2,256]{0,2,1:T(8,128)}), f32[2560,2,256]{0,2,1:T(8,128)}) %all-reduce.4.cloned.1.call-update) | async-done | bytes 5242896 | tf_op jit(solution)/shard_map/psum | solution.py:111
  375.8 9.2 %reduce_sum.29 = f32[3,256,256]{2,1,0:T(8,128)S(1)} reduce(f32[32,3,256,256]{3,2,1,0:T(8,128)} %bitcast.212, f32[]{:T(128)} %constant.211.clone.1), dimensions={0}, to_apply=%region_0.0 | reduce | flops 6094848 | bytes 25952260 | tf_op jit(solution)/shard_map/reduce_sum | solution.py:105
  386.5 4.8 gather_fusion
  391.6 11.7 %cholesky.130 = f32[128,128]{1,0:T(8,128)S(1)} custom-call(f32[128,128]{1,0:T(8,128)S(1)} %cholesky.194), custom_call_target="Cholesky" | custom-call | tf_op jit(solution)/shard_map/jit(cholesky)/cholesky | solution.py:31
  403.4 9.8 %custom-call.20 = f32[1,128,128]{1,2,0:T(8,128)S(1)} custom-call(f32[1,128,128]{2,1,0:T(8,128)S(1)} %get-tuple-element.87), custom_call_target="InvertDiagBlocksLowerTriangular" | custom-call | tf_op jit(solution)/shard_map/jit(cholesky)/cholesky | solution.py:31
  413.7 11.7 %cholesky.147 = f32[128,128]{1,0:T(8,128)S(1)} custom-call(f32[128,128]{1,0:T(8,128)S(1)} %convolution_subtract_fusion.6), custom_call_target="Cholesky" | custom-call | tf_op jit(solution)/shard_map/jit(cholesky)/cholesky | solution.py:31
  431.7 20.1 %custom-call.21 = f32[2,128,128]{1,2,0:T(8,128)S(1)} custom-call(f32[2,128,128]{2,1,0:T(8,128)S(1)} %get-tuple-element.41), custom_call_target="InvertDiagBlocksLowerTriangular" | custom-call | tf_op jit(solution)/shard_map/jit(_solve_triangular)/triangular_solve | solution.py:17
  463.3 5.8 fusion.8
  470.0 11.9 %cholesky.164 = f32[128,128]{1,0:T(8,128)S(1)} custom-call(f32[128,128]{1,0:T(8,128)S(1)} %cholesky.197), custom_call_target="Cholesky" | custom-call | tf_op jit(solution)/shard_map/jit(cholesky)/cholesky | solution.py:34
  481.9 9.8 %custom-call.22 = f32[1,128,128]{1,2,0:T(8,128)S(1)} custom-call(f32[1,128,128]{2,1,0:T(8,128)S(1)} %get-tuple-element.83), custom_call_target="InvertDiagBlocksLowerTriangular" | custom-call | tf_op jit(solution)/shard_map/jit(cholesky)/cholesky | solution.py:34
  493.9 11.7 %cholesky.181 = f32[128,128]{1,0:T(8,128)S(1)} custom-call(f32[128,128]{1,0:T(8,128)S(1)} %convolution_subtract_fusion.5), custom_call_target="Cholesky" | custom-call | tf_op jit(solution)/shard_map/jit(cholesky)/cholesky | solution.py:34
  513.0 20.5 %custom-call.23 = f32[2,128,128]{1,2,0:T(8,128)} custom-call(f32[2,128,128]{2,1,0:T(8,128)S(1)} %get-tuple-element.42), custom_call_target="InvertDiagBlocksLowerTriangular" | custom-call | tf_op jit(solution)/shard_map/jit(_solve_triangular)/triangular_solve | solution.py:17
  555.2 11.4 %convert_multiply_fusion = (f32[10,256,5,256]{1,3,2,0:T(8,128)}, f32[10,256,5,256]{1,3,2,0:T(8,128)}) fusion(bf16[10,1,256,5,1,256]{2,5,3,0,4,1:T(8,128)(2,1)} %copy.100, f32[10,5]{1,0:T(8,128)S(1)} %bitcast.217, pred[256,256]{0,1:T(8,128)(4,1)S(1)} %copy-done.10), kind=kLoop, calls=%fused_computation.8 | loop fusion | flops 9830400 | bytes 32833736 | tf_op jit(solution)/shard_map/mul | solution.py:141
  566.6 14.0 %copy.102 = f32[10,256,5,256]{3,1,2,0:T(8,128)} copy(f32[10,256,5,256]{1,3,2,0:T(8,128)} %get-tuple-element.67) | data formatting | bytes 26214400 | tf_op jit(solution)/shard_map/jit(tril)/select_n | solution.py:13
  580.6 14.2 %copy.105 = f32[10,256,5,256]{3,1,2,0:T(8,128)} copy(f32[10,256,5,256]{1,3,2,0:T(8,128)} %get-tuple-element.66) | data formatting | bytes 26214400 | tf_op jit(solution)/shard_map/mul | solution.py:141
  594.9 10.6 %copy.106 = f32[2560,2,256]{2,1,0:T(2,128)} copy(f32[2560,2,256]{2,0,1:T(8,128)} %copy-done) | data formatting | bytes 10485760 | tf_op jit(solution)/shard_map/scatter | solution.py:116
  605.6 8.0 %reshape.410 = f32[10,256,512,1]{2,1,0,3:T(8,128)} reshape(f32[2560,2,256]{2,1,0:T(2,128)} %copy.106) | data formatting | bytes 10485760 | tf_op jit(solution)/shard_map/dot_general | solution.py:124
  615.6 30.2 %fusion.6 = f32[10,1,256,5,1,256]{5,2,3,0,4,1:T(8,128)S(1)} fusion(f32[10,256,5,256]{3,1,2,0:T(8,128)} %copy.102, f32[10,256,5,256]{3,1,2,0:T(8,128)} %copy.105, bf16[10,1,256,5,1,256]{2,5,3,0,4,1:T(8,128)(2,1)} %copy.100, f32[10,256,256]{2,1,0:T(8,128)S(1)} %dynamic-slice_bitcast_fusion, pred[5]{0:T(512)(128)(4,1)S(1)} %broadcast_compare_fusion.3, ...), kind=kOutput, calls=%fused_computation.17 | convolution fusion | flops 20158873600 | bytes 56426652 | tf_op jit(solution)/shard_map/dot_general | solution.py:124
  645.8 15.0 %copy.108 = f32[10,1,256,5,1,256]{5,4,3,2,1,0:T(1,128)} copy(f32[10,1,256,5,1,256]{5,2,3,0,4,1:T(8,128)S(1)} %fusion.6) | data formatting | bytes 26214400 | tf_op jit(solution)/shard_map/reshape | solution.py:148
  (156 shorter events, 90.9 us)
Async XLA Ops:
  13.8 31.0 %all-to-all-start = ((f32[4,1,64]{2,1,0:T(1,128)}), f32[4,1,64]{2,1,0:T(1,128)S(1)}, u32[]{:S(2)}, u32[]{:S(2)}) async-start(f32[4,1,64]{2,1,0:T(1,128)} %all_to_all.9), calls=%async_computation | async-start | bytes 4096 | tf_op jit(solution)/shard_map/all_to_all | solution.py:88
  18.1 1.3 slice-start
  19.4 1.2 copy-start.9
  44.8 12.3 %all-to-all-start.1 = ((f32[4,64,2,256]{3,2,1,0:T(2,128)}), f32[4,64,2,256]{3,2,1,0:T(2,128)S(1)}, u32[]{:S(2)}, u32[]{:S(2)}) async-start(f32[4,64,2,256]{3,2,1,0:T(2,128)} %bitcast.27), calls=%async_computation.1 | async-start | bytes 1048576 | tf_op jit(solution)/shard_map/all_to_all | solution.py:81
  48.3 320.4 %all-reduce.4.cloned.1.call-start = ((), (), s32[]{:S(2)}) async-start(), calls=%async_computation.2 | async-start | bytes 10485760 | tf_op jit(solution)/shard_map/psum | solution.py:111
  96.9 2.2 copy-start.12
  96.9 278.9 %all-gather.3.cloned.1.call-start = ((), (), s32[]{:S(2)}) async-start(), calls=%async_computation.4 | async-start | bytes 25952256 | tf_op jit(solution)/shard_map/all_gather | solution.py:105
  99.0 516.6 %all-reduce.6.cloned.1.call-start = ((), (), s32[]{:S(2)}) async-start(), calls=%async_computation.3 | async-start | bytes 5242880 | tf_op jit(solution)/shard_map/psum | solution.py:9
  371.8 2.4 copy-start.1
  391.4 60.7 %copy-start.6 = (f32[512,512]{0,1:T(8,128)}, f32[512,512]{0,1:T(8,128)S(1)}, u32[]{:S(2)}) copy-start(f32[512,512]{0,1:T(8,128)S(1)} %select_add_fusion) | copy-start | bytes 3145732
  459.1 4.1 copy-start.2
  469.3 0.7 copy-start.8
  505.6 2.5 copy-start.7
  533.5 3.8 copy-start.4
  536.2 1.1 copy-start.3
  537.3 5.1 copy-start.11
  542.4 3.7 copy-start.5
  546.7 2.4 copy-start
  554.3 0.8 copy-start.10
Sparse Core Ops, SparseCore 0:
  97.0 271.6 all-reduce.3
  554.5 58.7 all-reduce.5
Sparse Core Ops, SparseCore 1:
  100.4 227.4 all-gather.2
